TPU v7x, 32 devices: a whole 2x2x4 slice. The times are simulated.
32 devices in a mesh: dom: 4 (over y, x), grp: 8 (over z, core).
Axes of the slice: x: 2, y: 2, z: 4, core: 2. Of those that a mesh axis runs over, the one named last changes fastest.
Arguments:
- features: bfloat16 [40960, 128], P(('dom', 'grp')), may hold values from -6 to 6
- send_dom: int32 [32, 4, 32], P(('dom', 'grp')), may hold values from 0 to 1279
- send_grp: int32 [32, 8, 32], P(('dom', 'grp')), may hold values from 0 to 1279
- tile_vals: bfloat16 [1536, 128, 128], P(('dom', 'grp')), may hold values from 0.049804688 to 1
- tile_tgt: int32 [1536], P(('dom', 'grp')), may hold values from 0 to 9, as said below
- tile_src: int32 [1536], P(('dom', 'grp')), may hold values from 0 to 12, as said below
- tile_count: int32 [32], P(('dom', 'grp')), may hold values from 13 to 48, as said below
- w_self: bfloat16 [128, 256], replicated, may hold values from -0.5 to 0.5
- w_neigh: bfloat16 [128, 256], replicated, may hold values from -0.5 to 0.5
- cotangent: bfloat16 [40960, 256], P(('dom', 'grp'))
Outputs:
- output: bfloat16 [40960, 256], P(('dom', 'grp'))
- grad_features: bfloat16 [40960, 128], P(('dom', 'grp'))
- grad_self: float32 [128, 256], replicated
- grad_neigh: float32 [128, 256], replicated
Inputs may be any that keep to these rules, and one draw needn't show every extreme that they name: `tile_tgt`: in every partition, tile slot t for t < 10 has target block t; other slots name any target block. `tile_src`: in every partition, tile slot t for t < 13 has source block t; other slots name any source block. `tile_count`: some partition has all 48 slots live in every draw.
All inputs are finite; a program needn't handle non-finite values.
Results may differ from a plain program's by a relative error of at most 0.0049.
Values may be sent and summed in bfloat16 or wider, within the bound.
No kernel may reach another device: no remote copies, remote signals or barrier semaphores. Data moves between devices by JAX's collectives and lax.ppermute only.
A program may use at most 64 MiB of HBM per device.

v0:
```python
import jax
import jax.numpy as jnp
from jax import lax
from jax.sharding import PartitionSpec as P


def per_device(
    features,
    send_dom,
    send_grp,
    tile_vals,
    tile_tgt,
    tile_src,
    tile_count,
    w_self,
    w_neigh,
    cotangent,
):
    tile_size = tile_vals.shape[1]
    width = features.shape[1]
    node_count = features.shape[0]
    block_count = node_count // tile_size
    dom_index = send_dom[0]
    grp_index = send_grp[0]
    dom_peers = dom_index.shape[0]
    recv_dom = lax.all_to_all(features[dom_index], "dom", split_axis=0, concat_axis=0, tiled=True)
    recv_grp = lax.all_to_all(features[grp_index], "grp", split_axis=0, concat_axis=0, tiled=True)
    source = jnp.concatenate(
        [features, recv_dom.reshape(-1, width), recv_grp.reshape(-1, width)], axis=0
    )
    source = source.reshape(-1, tile_size, width)
    source_count = source.shape[0]
    slot_count = tile_vals.shape[0]
    usable = jnp.arange(slot_count, dtype=jnp.int32) < tile_count[0]
    to_target = (
        (tile_tgt[None, :] == jnp.arange(block_count, dtype=jnp.int32)[:, None]) & usable[None, :]
    ).astype(jnp.float32)
    to_source = (
        (tile_src[None, :] == jnp.arange(source_count, dtype=jnp.int32)[:, None]) & usable[None, :]
    ).astype(jnp.float32)
    products = jnp.einsum(
        "tij,tjf->tif", tile_vals, source[tile_src], preferred_element_type=jnp.float32
    )
    summed = jnp.einsum("bt,tif->bif", to_target, products, precision=lax.Precision.HIGHEST)
    unit_column = jnp.ones((tile_size,), jnp.bfloat16)
    row_sums = jnp.einsum("tij,j->ti", tile_vals, unit_column, preferred_element_type=jnp.float32)
    degree = jnp.dot(to_target, row_sums, precision=lax.Precision.HIGHEST)
    agg = (summed / degree[:, :, None]).reshape(node_count, width).astype(jnp.bfloat16)
    preact = jnp.dot(features, w_self, preferred_element_type=jnp.float32) + jnp.dot(
        agg, w_neigh, preferred_element_type=jnp.float32
    )
    sigm = jax.nn.sigmoid(preact)
    output = (preact * sigm).astype(jnp.bfloat16)
    grad_pre = (cotangent.astype(jnp.float32) * sigm * (1.0 + preact * (1.0 - sigm))).astype(
        jnp.bfloat16
    )
    part_self = jnp.einsum("nf,nh->fh", features, grad_pre, preferred_element_type=jnp.float32)
    part_neigh = jnp.einsum("nf,nh->fh", agg, grad_pre, preferred_element_type=jnp.float32)
    grad_own = jnp.einsum("nh,fh->nf", grad_pre, w_self, preferred_element_type=jnp.float32)
    grad_agg = jnp.einsum("nh,fh->nf", grad_pre, w_neigh, preferred_element_type=jnp.float32)
    grad_agg = (grad_agg / degree.reshape(-1)[:, None]).astype(jnp.bfloat16)
    picked = grad_agg.reshape(block_count, tile_size, width)[tile_tgt]
    backward = jnp.einsum("tij,tif->tjf", tile_vals, picked, preferred_element_type=jnp.float32)
    grad_source = jnp.einsum(
        "st,tjf->sjf", to_source, backward, precision=lax.Precision.HIGHEST
    ).reshape(-1, width)
    dom_rows = dom_peers * dom_index.shape[1]
    back_dom = (
        grad_source[node_count : node_count + dom_rows]
        .reshape(dom_index.shape[0], dom_index.shape[1], width)
        .astype(jnp.bfloat16)
    )
    back_grp = (
        grad_source[node_count + dom_rows :]
        .reshape(grp_index.shape[0], grp_index.shape[1], width)
        .astype(jnp.bfloat16)
    )
    ret_dom = lax.all_to_all(back_dom, "dom", split_axis=0, concat_axis=0, tiled=True)
    ret_grp = lax.all_to_all(back_grp, "grp", split_axis=0, concat_axis=0, tiled=True)
    grad_self, grad_neigh = lax.psum((part_self, part_neigh), ("dom", "grp"))
    grad_total = grad_own + grad_source[:node_count]
    grad_total = grad_total.at[dom_index.reshape(-1)].add(
        ret_dom.reshape(-1, width).astype(jnp.float32)
    )
    grad_total = grad_total.at[grp_index.reshape(-1)].add(
        ret_grp.reshape(-1, width).astype(jnp.float32)
    )
    return (output, grad_total.astype(jnp.bfloat16), grad_self, grad_neigh)


def solution(mesh):
    return jax.shard_map(
        per_device,
        mesh=mesh,
        in_specs=(
            P(("dom", "grp"), None),
            P(("dom", "grp"), None, None),
            P(("dom", "grp"), None, None),
            P(("dom", "grp"), None, None),
            P(("dom", "grp")),
            P(("dom", "grp")),
            P(("dom", "grp")),
            P(),
            P(),
            P(("dom", "grp"), None),
        ),
        out_specs=(P(("dom", "grp"), None), P(("dom", "grp"), None), P(), P()),
        check_vma=False,
    )
```

profile of v0, /device:TPU:0, one launch (start us, length us, event | category | flops | bytes accessed | tf_op | source)
XLA Modules:
  0.0 210.0 jit_solution(4787525386066854471)
XLA Ops:
  7.2 0.8 compare_select_fusion.2
  8.1 2.3 %gather_fusion = bf16[128,128]{1,0:T(8,128)(2,1)} fusion(bf16[1280,128]{1,0:T(8,128)(2,1)} %param.10, s32[1024]{0:T(1024)S(1)} %pad_clamp_fusion.3), kind=kCustom, calls=%fused_computation | custom fusion | bytes 66048 | tf_op jit(solution)/shard_map/gather | solution.py:26
  10.4 5.2 %all-to-all-start = ((bf16[4,32,128]{2,1,0:T(8,128)(2,1)}), bf16[4,32,128]{2,1,0:T(8,128)(2,1)S(1)}, u32[]{:S(2)}, u32[]{:S(2)}) async-start(bf16[4,32,128]{2,1,0:T(8,128)(2,1)} %bitcast.3), calls=%async_computation | async-start | bytes 65536 | tf_op jit(solution)/shard_map/all_to_all | solution.py:26
  15.6 0.8 reshape_squeeze.6
  16.3 0.8 reshape_squeeze.7
  20.4 1.4 fusion.34
  21.9 1.5 gather_fusion.1
  23.4 4.9 %all-to-all-start.1 = ((bf16[8,32,128]{2,1,0:T(8,128)(2,1)}), bf16[8,32,128]{2,1,0:T(8,128)(2,1)S(1)}, u32[]{:S(2)}, u32[]{:S(2)}) async-start(bf16[8,32,128]{2,1,0:T(8,128)(2,1)} %bitcast.6), calls=%async_computation.1 | async-start | bytes 131072 | tf_op jit(solution)/shard_map/all_to_all | solution.py:27
  28.4 5.8 %all-to-all-done.1 = bf16[8,32,128]{2,1,0:T(8,128)(2,1)S(1)} async-done(((bf16[8,32,128]{2,1,0:T(8,128)(2,1)}), bf16[8,32,128]{2,1,0:T(8,128)(2,1)S(1)}, u32[]{:S(2)}, u32[]{:S(2)}) %all-to-all-start.1) | async-done | bytes 65568 | tf_op jit(solution)/shard_map/all_to_all | solution.py:27
  34.2 1.9 gather_fusion.2
  36.1 4.3 %fusion.35 = f32[48,128,128]{2,1,0:T(8,128)} fusion(bf16[48,128,128]{2,1,0:T(8,128)(2,1)} %gather_fusion.2, bf16[48,128,128]{2,1,0:T(8,128)(2,1)S(1)} %copy-done), kind=kOutput, calls=%fused_computation.55 | convolution fusion | flops 201326592 | bytes 6291456 | tf_op jit(solution)/shard_map/tij,tjf->tif/dot_general | solution.py:41
  40.4 3.6 %copy.22 = f32[48,128,128]{1,0,2:T(8,128)} copy(f32[48,128,128]{2,1,0:T(8,128)} %fusion.35) | data formatting | bytes 6291456 | tf_op jit(solution)/shard_map/tij,tjf->tif/dot_general | solution.py:41
  44.1 3.3 %fusion.8 = bf16[10,128,128]{2,0,1:T(8,128)(2,1)S(1)} fusion(f32[48,128,128]{1,0,2:T(8,128)} %copy.22, f32[10,128]{0,1:T(8,128)S(1)} %copy.17, s32[48]{0:T(128)S(1)} %copy-done.5, pred[48]{0:T(512)(128)(4,1)S(1)} %iota_compare_fusion.2), kind=kOutput, calls=%fused_computation.18 | convolution fusion | flops 94700480 | bytes 3478768 | tf_op jit(solution)/shard_map/bt,tif->bif/dot_general | solution.py:44
  47.5 1.6 multiply_convert_fusion
  49.1 1.0 fusion.37
  50.4 1.9 gather_fusion.3
  52.3 3.7 %fusion.36 = f32[48,128,128]{2,1,0:T(8,128)} fusion(bf16[48,128,128]{2,1,0:T(8,128)(2,1)} %gather_fusion.3, bf16[48,128,128]{2,1,0:T(8,128)(2,1)S(1)} %copy-done), kind=kOutput, calls=%fused_computation.56 | convolution fusion | flops 201326592 | bytes 6291456 | tf_op jit(solution)/shard_map/tij,tif->tjf/dot_general | solution.py:63
  56.1 3.6 %copy.24 = f32[48,128,128]{1,0,2:T(8,128)} copy(f32[48,128,128]{2,1,0:T(8,128)} %fusion.36) | data formatting | bytes 6291456 | tf_op jit(solution)/shard_map/tij,tif->tjf/dot_general | solution.py:63
  59.7 4.0 %fusion.33 = (bf16[13,128,128]{2,0,1:T(8,128)(2,1)S(1)}, f32[13,128,128]{2,0,1:T(8,128)}) fusion(f32[48,128,128]{1,0,2:T(8,128)} %copy.24, s32[48]{0:T(128)S(1)} %copy-done.6, pred[48]{0:T(512)(128)(4,1)S(1)} %iota_compare_fusion.2), kind=kOutput, calls=%fused_computation.53 | convolution fusion | flops 122897632 | bytes 4423920 | tf_op jit(solution)/shard_map/st,tjf->sjf/dot_general | solution.py:64
  64.4 4.2 %all-to-all-start.2 = ((bf16[4,32,128]{2,1,0:T(8,128)(2,1)}), bf16[4,32,128]{2,1,0:T(8,128)(2,1)S(1)}, u32[]{:S(2)}, u32[]{:S(2)}) async-start(bf16[4,32,128]{2,1,0:T(8,128)(2,1)} %bitcast.26), calls=%async_computation.2 | async-start | bytes 65536 | tf_op jit(solution)/shard_map/all_to_all | solution.py:78
  68.6 1.0 convolution_bitcast_fusion
  69.7 1.4 copy.19
  71.8 1.5 all-to-all-done.2
  73.4 3.4 %all-to-all-start.3 = ((bf16[8,32,128]{2,1,0:T(8,128)(2,1)}), bf16[8,32,128]{2,1,0:T(8,128)(2,1)S(1)}, u32[]{:S(2)}, u32[]{:S(2)}) async-start(bf16[8,32,128]{2,1,0:T(8,128)(2,1)} %bitcast.21), calls=%async_computation.3 | async-start | bytes 131072 | tf_op jit(solution)/shard_map/all_to_all | solution.py:79
  76.8 1.2 convolution_add_fusion.1
  77.9 3.1 %scatter_custom_fusion = f32[1280,128]{1,0:T(8,128)} fusion(f32[1280,128]{1,0:T(8,128)} %convolution_add_fusion.1, s32[128]{0:T(128)S(1)} %fusion.29, bf16[128,128]{1,0:T(8,128)(2,1)S(1)} %bitcast.80), kind=kCustom, calls=%fused_computation.23 | custom fusion | flops 32768 | bytes 688128 | tf_op jit(solution)/shard_map/scatter-add | solution.py:82
  81.0 1.6 all-to-all-done.3
  82.6 3.7 %scatter_custom_fusion.1 = f32[1280,128]{1,0:T(8,128)} fusion(f32[1280,128]{1,0:T(8,128)} %scatter_custom_fusion, s32[256]{0:T(256)S(1)} %bitcast.83, bf16[256,128]{1,0:T(8,128)(2,1)S(1)} %bitcast.77), kind=kCustom, calls=%fused_computation.21 | custom fusion | flops 65536 | bytes 720896 | tf_op jit(solution)/shard_map/scatter-add | solution.py:85
  86.3 1.8 convert_element_type.55
  88.1 111.7 %all-reduce.3.cloned.1.call-done = (f32[128,256]{0,1:T(8,128)}, f32[128,256]{1,0:T(8,128)}) async-done(((f32[128,256]{0,1:T(8,128)}, f32[128,256]{1,0:T(8,128)}), (f32[128,256]{0,1:T(8,128)}, f32[128,256]{1,0:T(8,128)})) %all-reduce.3.cloned.1.call-update) | async-done | bytes 262160 | tf_op jit(solution)/shard_map/psum | solution.py:80
  199.9 1.7 copy.21
  201.5 1.6 copy.31
  (43 shorter events, 4.9 us)
Async XLA Ops:
  7.2 12.7 %copy-start = (bf16[48,128,128]{2,1,0:T(8,128)(2,1)S(1)}, bf16[48,128,128]{2,1,0:T(8,128)(2,1)}, u32[]{:S(2)}) copy-start(bf16[48,128,128]{2,1,0:T(8,128)(2,1)} %param.13) | copy-start | bytes 4718596
  7.2 13.2 %copy-start.1 = (bf16[1280,128]{1,0:T(8,128)(2,1)S(1)}, bf16[1280,128]{1,0:T(8,128)(2,1)}, u32[]{:S(2)}) copy-start(bf16[1280,128]{1,0:T(8,128)(2,1)} %param.10) | copy-start | bytes 983044
  7.2 13.2 %copy-start.3 = (bf16[128,256]{1,0:T(8,128)(2,1)S(1)}, bf16[128,256]{1,0:T(8,128)(2,1)}, u32[]{:S(2)}) copy-start(bf16[128,256]{1,0:T(8,128)(2,1)} %param.17) | copy-start | bytes 196612
  10.4 13.0 %all-to-all-start = ((bf16[4,32,128]{2,1,0:T(8,128)(2,1)}), bf16[4,32,128]{2,1,0:T(8,128)(2,1)S(1)}, u32[]{:S(2)}, u32[]{:S(2)}) async-start(bf16[4,32,128]{2,1,0:T(8,128)(2,1)} %bitcast.3), calls=%async_computation | async-start | bytes 65536 | tf_op jit(solution)/shard_map/all_to_all | solution.py:26
  19.8 1.9 copy-start.5
  23.4 10.8 %all-to-all-start.1 = ((bf16[8,32,128]{2,1,0:T(8,128)(2,1)}), bf16[8,32,128]{2,1,0:T(8,128)(2,1)S(1)}, u32[]{:S(2)}, u32[]{:S(2)}) async-start(bf16[8,32,128]{2,1,0:T(8,128)(2,1)} %bitcast.6), calls=%async_computation.1 | async-start | bytes 131072 | tf_op jit(solution)/shard_map/all_to_all | solution.py:27
  44.1 3.4 %copy-start.2 = (f32[1280,256]{1,0:T(8,128)S(1)}, f32[1280,256]{1,0:T(8,128)}, u32[]{:S(2)}) copy-start(f32[1280,256]{1,0:T(8,128)} %fusion.34) | copy-start | bytes 3932164
  44.1 3.4 %copy-start.7 = (bf16[1280,256]{1,0:T(8,128)(2,1)S(1)}, bf16[1280,256]{1,0:T(8,128)(2,1)}, u32[]{:S(2)}) copy-start(bf16[1280,256]{1,0:T(8,128)(2,1)} %param.19) | copy-start | bytes 1966084
  44.1 3.4 %copy-start.8 = (bf16[128,256]{1,0:T(8,128)(2,1)S(1)}, bf16[128,256]{1,0:T(8,128)(2,1)}, u32[]{:S(2)}) copy-start(bf16[128,256]{1,0:T(8,128)(2,1)} %param.18) | copy-start | bytes 196612
  56.1 3.6 %copy-start.6 = (s32[48]{0:T(128)S(1)}, s32[48]{0:T(128)}, u32[]{:S(2)}) copy-start(s32[48]{0:T(128)} %param.15) | copy-start | bytes 580
  64.4 9.0 %all-to-all-start.2 = ((bf16[4,32,128]{2,1,0:T(8,128)(2,1)}), bf16[4,32,128]{2,1,0:T(8,128)(2,1)S(1)}, u32[]{:S(2)}, u32[]{:S(2)}) async-start(bf16[4,32,128]{2,1,0:T(8,128)(2,1)} %bitcast.26), calls=%async_computation.2 | async-start | bytes 65536 | tf_op jit(solution)/shard_map/all_to_all | solution.py:78
  68.6 8.1 %copy-start.4 = (bf16[128,256]{1,0:T(8,128)(2,1)S(1)}, bf16[128,256]{1,0:T(8,128)(2,1)}, u32[]{:S(2)}) copy-start(bf16[128,256]{1,0:T(8,128)(2,1)} %param.17) | copy-start | bytes 196612
  68.6 131.3 %all-reduce.3.cloned.1.call-start = ((), (), s32[]{:S(2)}) async-start(), calls=%async_computation.4 | async-start | bytes 524288 | tf_op jit(solution)/shard_map/psum | solution.py:80
  73.4 9.2 %all-to-all-start.3 = ((bf16[8,32,128]{2,1,0:T(8,128)(2,1)}), bf16[8,32,128]{2,1,0:T(8,128)(2,1)S(1)}, u32[]{:S(2)}, u32[]{:S(2)}) async-start(bf16[8,32,128]{2,1,0:T(8,128)(2,1)} %bitcast.21), calls=%async_computation.3 | async-start | bytes 131072 | tf_op jit(solution)/shard_map/all_to_all | solution.py:79
Sparse Core Ops, SparseCore 0:
  75.7 124.1 all-reduce.2
where the time goes:
time: 211 us; the launch traced here: 210 us
  waiting for transfers between devices  121 us (57%)
  local copies, waits for them, and re-layouts  22.9 us (11%)
  matrix products  22.5 us (11%)
  starting transfers between devices  17.6 us (8%)
  between operations  14.8 us (7%)
  other arithmetic  11.5 us (5%)
    psum x1, waiting for transfers between devices, per_device(): grad_self, grad_neigh = lax.psum((part_self, part_neigh), ('dom', 'grp'))  112 us
    all_to_all x1, waiting for transfers between devices, per_device(): lax.all_to_all(features[grp_index], 'grp', split_axis=0, concat_axis=0, t...  5.79 us
    all_to_all x1, starting transfers between devices, per_device(): lax.all_to_all(features[dom_index], 'dom', split_axis=0, concat_axis=0, t...  5.16 us
    all_to_all x1, starting transfers between devices, per_device(): lax.all_to_all(features[grp_index], 'grp', split_axis=0, concat_axis=0, t...  4.88 us
    dot_general x1, matrix products, per_device(): jnp.einsum('tij,tjf->tif', tile_vals, source[tile_src], preferred_element...  4.3 us
  transfers between devices with their start and end apart: 5, of which 4 were waited for; matrix products, arithmetic and copies ran while one was open for 10% of the time, Pallas kernels for 0%

commit v1 on v0

--- a/solution.py
+++ b/solution.py
@@ -2,6 +2,7 @@
 import jax.numpy as jnp
 from jax import lax
 from jax.sharding import PartitionSpec as P
+from jax.lax import psum
 
 
 def per_device(
@@ -77,7 +78,8 @@
     )
     ret_dom = lax.all_to_all(back_dom, "dom", split_axis=0, concat_axis=0, tiled=True)
     ret_grp = lax.all_to_all(back_grp, "grp", split_axis=0, concat_axis=0, tiled=True)
-    grad_self, grad_neigh = lax.psum((part_self, part_neigh), ("dom", "grp"))
+    unit_work = lambda q_in: psum(psum(q_in, axis_name="grp"), axis_name="dom")
+    grad_self, grad_neigh = unit_work((part_self, part_neigh))
     grad_total = grad_own + grad_source[:node_count]
     grad_total = grad_total.at[dom_index.reshape(-1)].add(
         ret_dom.reshape(-1, width).astype(jnp.float32)

time: 211 us -> 180 us (0.85)
  waiting for transfers between devices: 121 us -> 96.7 us
  other arithmetic: 11.5 us -> 7.36 us
  matrix products: 22.5 us -> 20.3 us
    psum x1 -> x2, waiting for transfers between devices: 112 us -> 87.4 us  [per_device(): unit_work = lambda q_in: psum(psum(q_in, axis_name='grp'), axis_name='dom')]
    unnamed x21 -> x27, local copies, waits for them, and re-layouts: 3.88 us -> 4.67 us
  transfers between devices with their start and end apart: 5 -> 6, of which waited for: 4 -> 4; matrix products, arithmetic and copies ran while one was open for 10% -> 8% of each run, Pallas kernels for 0% -> 0%
where the time goes in v1:
time: 180 us; the launch traced here: 179 us
  waiting for transfers between devices  96.7 us (54%)
  local copies, waits for them, and re-layouts  22.4 us (12%)
  matrix products  20.3 us (11%)
  starting transfers between devices  17.6 us (10%)
  between operations  14.9 us (8%)
  other arithmetic  7.36 us (4%)
    psum x2, waiting for transfers between devices, per_device(): unit_work = lambda q_in: psum(psum(q_in, axis_name='grp'), axis_name='dom')  87.4 us
    all_to_all x1, waiting for transfers between devices, per_device(): lax.all_to_all(features[grp_index], 'grp', split_axis=0, concat_axis=0, t...  5.7 us
    all_to_all x1, starting transfers between devices, per_device(): lax.all_to_all(features[dom_index], 'dom', split_axis=0, concat_axis=0, t...  5.16 us
    all_to_all x1, starting transfers between devices, per_device(): lax.all_to_all(features[grp_index], 'grp', split_axis=0, concat_axis=0, t...  4.88 us
    unnamed x27, local copies, waits for them, and re-layouts  4.67 us
    dot_general x1, matrix products, per_device(): jnp.einsum('tij,tjf->tif', tile_vals, source[tile_src], preferred_element...  4.31 us
    all_to_all x1, starting transfers between devices, per_device(): lax.all_to_all(back_dom, 'dom', split_axis=0, concat_axis=0, tiled=True)  4.19 us
    dot_general x1, local copies, waits for them, and re-layouts, per_device(): jnp.einsum('tij,tif->tjf', tile_vals, picked, preferred_element_type=jnp....  3.62 us
  transfers between devices with their start and end apart: 6, of which 4 were waited for; matrix products, arithmetic and copies ran while one was open for 8% of the time, Pallas kernels for 0%

profile of v1, /device:TPU:0, one launch (start us, length us, event | category | flops | bytes accessed | tf_op | source)
XLA Modules:
  0.0 179.4 jit_solution(8764340925082521782)
XLA Ops:
  7.2 0.8 compare_select_fusion.2
  8.1 2.3 %gather_fusion = bf16[128,128]{1,0:T(8,128)(2,1)} fusion(bf16[1280,128]{1,0:T(8,128)(2,1)} %param.10, s32[1024]{0:T(1024)S(1)} %pad_clamp_fusion.3), kind=kCustom, calls=%fused_computation | custom fusion | bytes 66048 | tf_op jit(solution)/shard_map/gather | solution.py:27
  10.4 5.2 %all-to-all-start = ((bf16[4,32,128]{2,1,0:T(8,128)(2,1)}), bf16[4,32,128]{2,1,0:T(8,128)(2,1)S(1)}, u32[]{:S(2)}, u32[]{:S(2)}) async-start(bf16[4,32,128]{2,1,0:T(8,128)(2,1)} %bitcast.3), calls=%async_computation | async-start | bytes 65536 | tf_op jit(solution)/shard_map/all_to_all | solution.py:27
  15.6 0.8 reshape_squeeze.7
  19.6 1.4 fusion.34
  21.1 1.5 gather_fusion.1
  22.6 4.9 %all-to-all-start.1 = ((bf16[8,32,128]{2,1,0:T(8,128)(2,1)}), bf16[8,32,128]{2,1,0:T(8,128)(2,1)S(1)}, u32[]{:S(2)}, u32[]{:S(2)}) async-start(bf16[8,32,128]{2,1,0:T(8,128)(2,1)} %bitcast.6), calls=%async_computation.1 | async-start | bytes 131072 | tf_op jit(solution)/shard_map/all_to_all | solution.py:28
  27.7 5.7 %all-to-all-done.1 = bf16[8,32,128]{2,1,0:T(8,128)(2,1)S(1)} async-done(((bf16[8,32,128]{2,1,0:T(8,128)(2,1)}), bf16[8,32,128]{2,1,0:T(8,128)(2,1)S(1)}, u32[]{:S(2)}, u32[]{:S(2)}) %all-to-all-start.1) | async-done | bytes 65568 | tf_op jit(solution)/shard_map/all_to_all | solution.py:28
  33.4 2.0 %gather_fusion.2 = bf16[48,128,128]{2,1,0:T(8,128)(2,1)} fusion(bf16[13,128,128]{2,1,0:T(8,128)(2,1)S(1)} %bitcast.71, s32[1024]{0:T(1024)S(1)} %pad_clamp_fusion.1), kind=kCustom, calls=%fused_computation.2 | custom fusion | bytes 3145920 | tf_op jit(solution)/shard_map/gather | solution.py:43
  35.4 4.3 %fusion.35 = f32[48,128,128]{2,1,0:T(8,128)} fusion(bf16[48,128,128]{2,1,0:T(8,128)(2,1)} %gather_fusion.2, bf16[48,128,128]{2,1,0:T(8,128)(2,1)S(1)} %copy-done), kind=kOutput, calls=%fused_computation.55 | convolution fusion | flops 201326592 | bytes 6291456 | tf_op jit(solution)/shard_map/tij,tjf->tif/dot_general | solution.py:42
  39.7 3.6 %copy.22 = f32[48,128,128]{1,0,2:T(8,128)} copy(f32[48,128,128]{2,1,0:T(8,128)} %fusion.35) | data formatting | bytes 6291456 | tf_op jit(solution)/shard_map/tij,tjf->tif/dot_general | solution.py:42
  43.3 3.3 %fusion.8 = bf16[10,128,128]{2,0,1:T(8,128)(2,1)S(1)} fusion(f32[48,128,128]{1,0,2:T(8,128)} %copy.22, f32[10,128]{0,1:T(8,128)S(1)} %copy.17, s32[48]{0:T(128)S(1)} %copy-done.8, pred[48]{0:T(512)(128)(4,1)S(1)} %iota_compare_fusion.2), kind=kOutput, calls=%fused_computation.18 | convolution fusion | flops 94700480 | bytes 3478768 | tf_op jit(solution)/shard_map/bt,tif->bif/dot_general | solution.py:45
  46.7 1.7 multiply_convert_fusion
  48.3 1.0 fusion.37
  49.3 1.0 convolution_bitcast_fusion
  50.7 0.8 gather_fusion.3
  51.5 2.3 %fusion.36 = f32[48,128,128]{2,1,0:T(8,128)} fusion(bf16[48,128,128]{2,1,0:T(8,128)(2,1)S(1)} %gather_fusion.3, bf16[48,128,128]{2,1,0:T(8,128)(2,1)S(1)} %copy-done), kind=kOutput, calls=%fused_computation.56 | convolution fusion | flops 201326592 | bytes 6291456 | tf_op jit(solution)/shard_map/tij,tif->tjf/dot_general | solution.py:64
  53.9 3.6 %copy.24 = f32[48,128,128]{1,0,2:T(8,128)} copy(f32[48,128,128]{2,1,0:T(8,128)} %fusion.36) | data formatting | bytes 6291456 | tf_op jit(solution)/shard_map/tij,tif->tjf/dot_general | solution.py:64
  57.5 3.0 %fusion.33 = (bf16[13,128,128]{2,0,1:T(8,128)(2,1)S(1)}, f32[13,128,128]{2,0,1:T(8,128)S(1)}) fusion(f32[48,128,128]{1,0,2:T(8,128)} %copy.24, s32[48]{0:T(128)S(1)} %copy-done.9, pred[48]{0:T(512)(128)(4,1)S(1)} %iota_compare_fusion.2), kind=kOutput, calls=%fused_computation.53 | convolution fusion | flops 122897632 | bytes 4423920 | tf_op jit(solution)/shard_map/st,tjf->sjf/dot_general | solution.py:65
  60.6 0.8 copy-done.5
  62.1 4.2 %all-to-all-start.2 = ((bf16[4,32,128]{2,1,0:T(8,128)(2,1)}), bf16[4,32,128]{2,1,0:T(8,128)(2,1)S(1)}, u32[]{:S(2)}, u32[]{:S(2)}) async-start(bf16[4,32,128]{2,1,0:T(8,128)(2,1)} %bitcast.26), calls=%async_computation.2 | async-start | bytes 65536 | tf_op jit(solution)/shard_map/all_to_all | solution.py:79
  67.0 1.0 slice.30
  68.0 1.0 copy.19
  69.7 54.4 %all-reduce.5.cloned.1.call-done = (f32[128,256]{0,1:T(8,128)}, f32[128,256]{1,0:T(8,128)}) async-done(((f32[128,256]{0,1:T(8,128)}, f32[128,256]{1,0:T(8,128)}), (f32[128,256]{0,1:T(8,128)}, f32[128,256]{1,0:T(8,128)})) %all-reduce.5.cloned.1.call-update) | async-done | bytes 262160 | tf_op jit(solution)/shard_map/psum | solution.py:81
  124.1 3.4 %all-to-all-start.3 = ((bf16[8,32,128]{2,1,0:T(8,128)(2,1)}), bf16[8,32,128]{2,1,0:T(8,128)(2,1)S(1)}, u32[]{:S(2)}, u32[]{:S(2)}) async-start(bf16[8,32,128]{2,1,0:T(8,128)(2,1)} %bitcast.21), calls=%async_computation.3 | async-start | bytes 131072 | tf_op jit(solution)/shard_map/all_to_all | solution.py:80
  127.5 1.4 convolution_add_fusion.1
  128.9 1.5 scatter_custom_fusion
  130.5 2.9 %all-to-all-done.3 = bf16[8,32,128]{2,1,0:T(8,128)(2,1)S(1)} async-done(((bf16[8,32,128]{2,1,0:T(8,128)(2,1)}), bf16[8,32,128]{2,1,0:T(8,128)(2,1)S(1)}, u32[]{:S(2)}, u32[]{:S(2)}) %all-to-all-start.3) | async-done | bytes 65568 | tf_op jit(solution)/shard_map/all_to_all | solution.py:80
  133.4 2.2 %scatter_custom_fusion.1 = f32[1280,128]{1,0:T(8,128)S(1)} fusion(f32[1280,128]{1,0:T(8,128)S(1)} %scatter_custom_fusion, s32[256]{0:T(256)S(1)} %bitcast.83, bf16[256,128]{1,0:T(8,128)(2,1)S(1)} %bitcast.77), kind=kCustom, calls=%fused_computation.21 | custom fusion | flops 65536 | bytes 720896 | tf_op jit(solution)/shard_map/scatter-add | solution.py:87
  136.3 33.0 %all-reduce.7.cloned.1.call-done = (f32[128,256]{0,1:T(8,128)}, f32[128,256]{1,0:T(8,128)}) async-done(((f32[128,256]{0,1:T(8,128)}, f32[128,256]{1,0:T(8,128)}), (f32[128,256]{0,1:T(8,128)}, f32[128,256]{1,0:T(8,128)})) %all-reduce.7.cloned.1.call-update) | async-done | bytes 262160 | tf_op jit(solution)/shard_map/psum | solution.py:81
  169.4 1.7 copy.21
  171.0 1.6 copy.33
  (52 shorter events, 6.4 us)
Async XLA Ops:
  7.2 11.9 %copy-start = (bf16[48,128,128]{2,1,0:T(8,128)(2,1)S(1)}, bf16[48,128,128]{2,1,0:T(8,128)(2,1)}, u32[]{:S(2)}) copy-start(bf16[48,128,128]{2,1,0:T(8,128)(2,1)} %param.13) | copy-start | bytes 4718596
  7.2 12.4 %copy-start.1 = (bf16[1280,128]{1,0:T(8,128)(2,1)S(1)}, bf16[1280,128]{1,0:T(8,128)(2,1)}, u32[]{:S(2)}) copy-start(bf16[1280,128]{1,0:T(8,128)(2,1)} %param.10) | copy-start | bytes 983044
  7.2 12.4 %copy-start.6 = (bf16[128,256]{1,0:T(8,128)(2,1)S(1)}, bf16[128,256]{1,0:T(8,128)(2,1)}, u32[]{:S(2)}) copy-start(bf16[128,256]{1,0:T(8,128)(2,1)} %param.17) | copy-start | bytes 196612
  10.4 12.2 %all-to-all-start = ((bf16[4,32,128]{2,1,0:T(8,128)(2,1)}), bf16[4,32,128]{2,1,0:T(8,128)(2,1)S(1)}, u32[]{:S(2)}, u32[]{:S(2)}) async-start(bf16[4,32,128]{2,1,0:T(8,128)(2,1)} %bitcast.3), calls=%async_computation | async-start | bytes 65536 | tf_op jit(solution)/shard_map/all_to_all | solution.py:27
  19.1 1.9 %copy-start.8 = (s32[48]{0:T(128)S(1)}, s32[48]{0:T(128)}, u32[]{:S(2)}) copy-start(s32[48]{0:T(128)} %param.14) | copy-start | bytes 580
  19.6 7.9 %copy-start.7 = (s32[1,4,32]{2,1,0:T(4,128)S(1)}, s32[1,4,32]{2,1,0:T(4,128)}, u32[]{:S(2)}) copy-start(s32[1,4,32]{2,1,0:T(4,128)} %param.11) | copy-start | bytes 1540
  22.6 10.8 %all-to-all-start.1 = ((bf16[8,32,128]{2,1,0:T(8,128)(2,1)}), bf16[8,32,128]{2,1,0:T(8,128)(2,1)S(1)}, u32[]{:S(2)}, u32[]{:S(2)}) async-start(bf16[8,32,128]{2,1,0:T(8,128)(2,1)} %bitcast.6), calls=%async_computation.1 | async-start | bytes 131072 | tf_op jit(solution)/shard_map/all_to_all | solution.py:28
  43.3 3.4 %copy-start.4 = (f32[1280,256]{1,0:T(8,128)S(1)}, f32[1280,256]{1,0:T(8,128)}, u32[]{:S(2)}) copy-start(f32[1280,256]{1,0:T(8,128)} %fusion.34) | copy-start | bytes 3932164
  43.3 3.4 %copy-start.10 = (bf16[1280,256]{1,0:T(8,128)(2,1)S(1)}, bf16[1280,256]{1,0:T(8,128)(2,1)}, u32[]{:S(2)}) copy-start(bf16[1280,256]{1,0:T(8,128)(2,1)} %param.19) | copy-start | bytes 1966084
  43.3 3.4 %copy-start.11 = (bf16[128,256]{1,0:T(8,128)(2,1)S(1)}, bf16[128,256]{1,0:T(8,128)(2,1)}, u32[]{:S(2)}) copy-start(bf16[128,256]{1,0:T(8,128)(2,1)} %param.18) | copy-start | bytes 196612
  48.3 2.3 %copy-start.2 = (bf16[1280,256]{1,0:T(8,128)(2,1)}, bf16[1280,256]{1,0:T(8,128)(2,1)S(1)}, u32[]{:S(2)}) copy-start(bf16[1280,256]{1,0:T(8,128)(2,1)S(1)} %get-tuple-element.16) | copy-start | bytes 1966084
  53.9 3.6 %copy-start.9 = (s32[48]{0:T(128)S(1)}, s32[48]{0:T(128)}, u32[]{:S(2)}) copy-start(s32[48]{0:T(128)} %param.15) | copy-start | bytes 580
  60.6 0.8 copy-start.5
  60.6 66.9 %copy-start.3 = (bf16[1280,256]{1,0:T(8,128)(2,1)S(1)}, bf16[1280,256]{1,0:T(8,128)(2,1)}, u32[]{:S(2)}) copy-start(bf16[1280,256]{1,0:T(8,128)(2,1)} %copy-done.2) | copy-start | bytes 1966084
  62.1 62.1 %all-to-all-start.2 = ((bf16[4,32,128]{2,1,0:T(8,128)(2,1)}), bf16[4,32,128]{2,1,0:T(8,128)(2,1)S(1)}, u32[]{:S(2)}, u32[]{:S(2)}) async-start(bf16[4,32,128]{2,1,0:T(8,128)(2,1)} %bitcast.26), calls=%async_computation.2 | async-start | bytes 65536 | tf_op jit(solution)/shard_map/all_to_all | solution.py:79
  66.2 57.9 %all-reduce.5.cloned.1.call-start = ((), (), s32[]{:S(2)}) async-start(), calls=%async_computation.4 | async-start | bytes 524288 | tf_op jit(solution)/shard_map/psum | solution.py:81
  67.0 102.4 %all-reduce.7.cloned.1.call-start = ((), (), s32[]{:S(2)}) async-start(), calls=%async_computation.5 | async-start | bytes 524288 | tf_op jit(solution)/shard_map/psum | solution.py:81
  124.1 9.2 %all-to-all-start.3 = ((bf16[8,32,128]{2,1,0:T(8,128)(2,1)}), bf16[8,32,128]{2,1,0:T(8,128)(2,1)S(1)}, u32[]{:S(2)}, u32[]{:S(2)}) async-start(bf16[8,32,128]{2,1,0:T(8,128)(2,1)} %bitcast.21), calls=%async_computation.3 | async-start | bytes 131072 | tf_op jit(solution)/shard_map/all_to_all | solution.py:80
Sparse Core Ops, SparseCore 0:
  70.0 54.0 all-reduce.4
  127.3 42.0 all-reduce.6
